TPU v7x, 128 devices: a whole 4x4x4 slice. The times are simulated.
128 devices in a mesh: valve: 8 (over y, core), bulk: 16 (over z, x).
Axes of the slice: x: 4, y: 4, z: 4, core: 2. Of those that a mesh axis runs over, the one named last changes fastest.
Arguments:
- solution: float32 [5, 64, 131072], P(None, None, ('valve', 'bulk')), may hold values from -6 to 6
- velocity: float32 [3, 131072], P(None, ('valve', 'bulk')), may hold values from -1 to 1
- inv_jacobian: float32 [64, 131072], P(None, ('valve', 'bulk')), may hold values from 0.5 to 3
- face_speed: float32 [96, 131072], P(None, ('valve', 'bulk')), may hold values from -6 to 6
- face_link: int32 [6, 131072], P(None, ('valve', 'bulk')), may hold values from 0 to 6271, as said below
- donor_elem: int32 [1048576], P(('valve', 'bulk')), may hold values from 0 to 1023
- ref_coords: float32 [3, 1048576], P(None, ('valve', 'bulk')), may hold values from -1 to 1
- owner_list: int32 [1048576, 1], P(('valve', 'bulk')), may hold values from 0 to 15; in each aligned block of 8192 rows (0 to 8191, 8192 to 16383, ...) at most 1024 rows name the same one
Outputs:
- section_rate: float32 [5, 64, 131072], P(None, None, ('valve', 'bulk'))
- fringe_values: float32 [5, 2097152], P(None, ('valve', 'bulk'))
Inputs may be any that keep to these rules, and one draw needn't show every extreme that they name: `face_link`: on each device, the values 6 * 1024 to 6271 appear exactly once each; every other face slot links to another slot of the same device that links back to it. `owner_list`: among the receptors of one device no owner is named more than 1024 times; in every draw some device names some owner exactly 1024 times.
All inputs are finite; a program needn't handle non-finite values.
Results may differ from a plain program's by a relative error of at most 0.0003.
Values sent between devices are 32-bit elements; how exact they have to be, the bound alone decides.
No kernel may reach another device: no remote copies, remote signals or barrier semaphores. Data moves between devices by JAX's collectives and lax.ppermute only.
A program may use at most 192 MiB of HBM per device.

v0:
```python
import jax
import jax.numpy as jnp
import numpy as np
from jax import lax
from jax.sharding import PartitionSpec as P

gauss_nodes = (-0.8611363115940526, -0.3399810435848563, 0.3399810435848563, 0.8611363115940526)
quad_weights = (0.3478548451374538, 0.6521451548625461, 0.6521451548625461, 0.3478548451374538)
section_step = 0.2


def padded(shard, sides, width):
    for axis, dim in sides:
        size, length = (lax.axis_size(axis), shard.shape[dim])
        up = [(i, (i + 1) % size) for i in range(size)]
        down = [(j, i) for i, j in up]
        last = lax.slice_in_dim(shard, length - width, length, axis=dim)
        initial = lax.slice_in_dim(shard, 0, width, axis=dim)
        before = lax.ppermute(last, axis, up)
        after = lax.ppermute(initial, axis, down)
        shard = jnp.concatenate([before, shard, after], axis=dim)
    return shard


def lagrange_at(x):
    values = []
    for j in range(4):
        factor = 1.0
        for m in range(4):
            if m != j:
                factor = factor * (x - gauss_nodes[m]) / (gauss_nodes[j] - gauss_nodes[m])
        values.append(factor)
    return values


def tables():
    slopes = np.zeros((4, 4))
    for i in range(4):
        for j in range(4):
            summed = 0.0
            for m in range(4):
                if m != j:
                    product = 1.0 / (gauss_nodes[j] - gauss_nodes[m])
                    for n in range(4):
                        if n != j and n != m:
                            product = (
                                product
                                * (gauss_nodes[i] - gauss_nodes[n])
                                / (gauss_nodes[j] - gauss_nodes[n])
                            )
                    summed = summed + product
            slopes[i, j] = summed
    end_values = [lagrange_at(-1.0), lagrange_at(1.0)]
    extrapolate = np.zeros((96, 64))
    lifting = np.zeros((64, 96))
    derivative = np.zeros((3, 64, 64))
    for p in range(64):
        point_idx = (p // 16, p // 4 % 4, p % 4)
        for f in range(6):
            normal_dir = f // 2
            across = [t for t in range(3) if t != normal_dir]
            q = point_idx[across[0]] * 4 + point_idx[across[1]]
            flux_row = q * 6 + f
            extrapolate[flux_row, p] = end_values[f % 2][point_idx[normal_dir]]
            lifting[p, flux_row] = (
                end_values[f % 2][point_idx[normal_dir]] / quad_weights[point_idx[normal_dir]]
            )
        for s in range(64):
            other_idx = (s // 16, s // 4 % 4, s % 4)
            for normal_dir in range(3):
                if all((point_idx[t] == other_idx[t] for t in range(3) if t != normal_dir)):
                    derivative[normal_dir, p, s] = slopes[
                        point_idx[normal_dir], other_idx[normal_dir]
                    ]
    return (
        jnp.asarray(extrapolate, dtype=jnp.float32),
        jnp.asarray(derivative, dtype=jnp.float32),
        jnp.asarray(lifting, dtype=jnp.float32),
    )


def face_rows(solution, face_speed, extrapolate):
    nvars = solution.shape[0]
    elems = solution.shape[2]
    ext_faces = extrapolate.reshape(16, 6, 64)
    values = jnp.einsum("qfp,vpe->feqv", ext_faces, solution, precision=lax.Precision.HIGHEST)
    values = values.reshape(6 * elems, 16, nvars)
    speeds = jnp.transpose(face_speed.reshape(16, 6, elems), (1, 2, 0)).reshape(6 * elems, 16)
    return (values, speeds)


def rim_rows(table_own, links, faces_total, rim_count):
    slots = jnp.where(links >= faces_total, links - faces_total, 2 * rim_count)
    senders = (
        jnp.zeros((2 * rim_count,), jnp.int32)
        .at[slots]
        .set(jnp.arange(faces_total, dtype=jnp.int32), mode="drop")
    )
    return jnp.take(table_own, senders, axis=0)


def surface_term(values, speeds, table_own, links, received, lifting, elems):
    nvars = values.shape[2]
    full_table = jnp.concatenate([table_own, received], axis=0)
    outer = jnp.take(full_table, links, axis=0)
    outer_vals = outer[:, : 16 * nvars].reshape(6 * elems, 16, nvars)
    outer_speed = outer[:, 16 * nvars :][:, :, None]
    own_speed = speeds[:, :, None]
    normal = 0.5 * (own_speed - outer_speed)
    common = 0.5 * normal * (values + outer_vals) + 0.5 * jnp.abs(normal) * (values - outer_vals)
    jump_term = (common - own_speed * values).reshape(6, elems, 16, nvars)
    lift_faces = lifting.reshape(64, 16, 6)
    return jnp.einsum("pqf,feqv->vpe", lift_faces, jump_term, precision=lax.Precision.HIGHEST)


def volume_term(solution, velocity, derivative):
    slopes = jnp.einsum("dpq,vqe->dvpe", derivative, solution, precision=lax.Precision.HIGHEST)
    return jnp.sum(velocity[:, None, None, :] * slopes, axis=0)


def receptor_rows(advanced, donors, coords):
    nvars = advanced.shape[0]
    elems = advanced.shape[2]
    basis_x = jnp.stack(lagrange_at(coords[0]))
    basis_y = jnp.stack(lagrange_at(coords[1]))
    basis_z = jnp.stack(lagrange_at(coords[2]))
    weights = (
        basis_x[:, None, None, :] * basis_y[None, :, None, :] * basis_z[None, None, :, :]
    ).reshape(64, -1)
    element_rows = jnp.transpose(advanced, (2, 0, 1)).reshape(elems, nvars * 64)
    picked = jnp.take(element_rows, donors, axis=0).reshape(donors.shape[0], nvars, 64)
    return jnp.einsum("rvp,pr->rv", picked, weights, precision=lax.Precision.HIGHEST)


def on_device(
    solution, velocity, inv_jacobian, face_speed, face_link, donor_elem, ref_coords, owner_list
):
    extrapolate, derivative, lifting = tables()
    nvars = solution.shape[0]
    elems = solution.shape[2]
    rim_count = elems // 16
    faces_total = 6 * elems
    links = face_link.reshape(faces_total)
    values, speeds = face_rows(solution, face_speed, extrapolate)
    table_own = jnp.concatenate([values.reshape(faces_total, 16 * nvars), speeds], axis=1)
    outgoing = rim_rows(table_own, links, faces_total, rim_count)
    extended = padded(outgoing, (("valve", 0),), rim_count)
    received = jnp.concatenate([extended[:rim_count], extended[3 * rim_count :]], axis=0)
    surface = surface_term(values, speeds, table_own, links, received, lifting, elems)
    volume = volume_term(solution, velocity, derivative)
    section_rate = -inv_jacobian[None] * (volume + surface)
    advanced = solution + section_step * section_rate
    receptor_vals = receptor_rows(advanced, donor_elem, ref_coords)
    buckets = lax.axis_size("bulk")
    receptors = receptor_vals.shape[0]
    capacity = 2 * receptors // buckets
    owners = owner_list[:, 0]
    gathered_vals, gathered_owners = (
        lax.all_gather(receptor_vals, "bulk", axis=0, tiled=True),
        lax.all_gather(owners, "bulk", axis=0, tiled=True),
    )
    by_source = gathered_owners.reshape(buckets, receptors)
    matches = (by_source == lax.axis_index("bulk")).astype(jnp.int32)
    before = jnp.cumsum(matches, axis=1) - matches
    places = jnp.where(
        matches == 1,
        jnp.arange(buckets, dtype=jnp.int32)[:, None] * capacity + before,
        buckets * capacity,
    ).reshape(buckets * receptors)
    fringe_rows = jnp.zeros((buckets * capacity, nvars), jnp.float32)
    fringe_rows = fringe_rows.at[places].set(gathered_vals, mode="drop")
    return (section_rate, jnp.transpose(fringe_rows))


def solution(mesh):
    placed = (
        P(None, None, ("valve", "bulk")),
        P(None, ("valve", "bulk")),
        P(None, ("valve", "bulk")),
        P(None, ("valve", "bulk")),
        P(None, ("valve", "bulk")),
        P(("valve", "bulk")),
        P(None, ("valve", "bulk")),
        P(("valve", "bulk"), None),
    )
    return jax.shard_map(
        on_device,
        mesh=mesh,
        in_specs=placed,
        out_specs=(P(None, None, ("valve", "bulk")), P(None, ("valve", "bulk"))),
        check_vma=False,
    )
```

profile of v0, /device:TPU:1, one launch (start us, length us, event | category | flops | bytes accessed | tf_op | source)
XLA Modules:
  0.0 905.8 jit_solution(7143843174503303031)
XLA Ops:
  7.2 0.8 copy.45
  8.1 23.0 %scatter_custom_fusion = s32[128]{0:T(128)S(1)} fusion(s32[6144]{0:T(1024)S(1)} %bitcast.87, s32[6144]{0:T(1024)S(1)} %iota.8, s32[]{:T(128)} %constant.125.clone.1), kind=kCustom, calls=%fused_computation.82 | custom fusion | bytes 516 | tf_op jit(solution)/shard_map/scatter | solution.py:97
  31.1 1.8 reshape.165
  33.0 1.9 copy.19
  34.9 4.0 convolution_bitcast_fusion
  38.9 1.2 copy.20
  40.1 2.5 copy.44
  42.6 3.4 copy.21
  46.1 4.6 pad_maximum_fusion.1
  50.6 2.6 gather_fusion
  53.3 2.7 collective-permute-start
  56.1 0.6 fusion.25
  56.8 0.8 multiply_multiply_fusion.11
  57.5 0.2 pad_maximum_fusion.2
  57.8 0.1 broadcast_multiply_fusion.2
  58.0 4.4 multiply_reduce_fusion.1
  62.3 0.1 pad_maximum_fusion.4
  62.5 0.5 broadcast_multiply_fusion.1
  63.0 22.0 %all-gather = s32[131072,1]{0,1:T(1,128)} all-gather(s32[8192,1]{0,1:T(1,128)S(1)} %copy-done.16), channel_id=2, replica_groups=mesh['valve'=8,'bulk'=16] {'bulk'}, dimensions={0}, use_global_device_ids=true | all-gather | bytes 557056 | tf_op jit(solution)/shard_map/all_gather | solution.py:160
  85.0 1.0 copy.27
  86.0 2.0 mul.255
  88.0 0.6 copy-done.15
  88.6 3.8 pad_maximum_fusion
  92.3 21.1 %gather_fusion.1 = f32[6144,96]{1,0:T(8,128)} fusion(f32[6272,96]{1,0:T(8,128)S(1)} %pad_maximum_fusion, s32[6144]{0:T(1024)S(1)} %broadcast_clamp_fusion), kind=kCustom, calls=%fused_computation.1 | custom fusion | bytes 4743168 | tf_op jit(solution)/shard_map/jit(_take)/gather | solution.py:105
  113.4 4.8 broadcast_select_fusion
  118.2 3.5 broadcast_multiply_fusion
  121.7 2.2 copy.23
  123.8 3.4 reshape.169
  127.2 3.2 copy.22
  130.4 3.0 copy.25
  133.4 7.4 multiply_add_fusion
  140.8 1.8 copy.29
  142.6 34.8 %gather_fusion.2 = f32[8192,320]{1,0:T(8,128)} fusion(f32[1024,320]{1,0:T(8,128)S(1)} %copy.29, s32[8192]{0:T(1024)} %fusion.25), kind=kCustom, calls=%fused_computation.2 | custom fusion | bytes 21004288 | tf_op jit(solution)/shard_map/jit(_take)/gather | solution.py:131
  177.5 12.1 %copy.30 = f32[8192,320]{0,1:T(8,128)} copy(f32[8192,320]{1,0:T(8,128)} %gather_fusion.2) | data formatting | bytes 20971520 | tf_op jit(solution)/shard_map/jit(_take)/gather | solution.py:131
  189.5 5.7 multiply_reduce_fusion
  195.2 2.7 copy.42
  197.9 1.0 copy-done.8
  199.0 0.5 compare_convert_fusion
  199.4 0.1 broadcast_bitcast_fusion
  199.5 0.1 copy.46
  199.6 5.0 reduce-window.6
  204.6 0.5 slice_reduce_fusion
  205.2 0.2 reduce-window.9
  205.4 0.2 broadcast_add_fusion
  205.6 0.1 compare_select_fusion
  205.7 365.4 %all-gather.3.cloned.1.call-done = f32[131072,5]{1,0:T(8,128)} async-done(((f32[8192,5]{1,0:T(8,128)}), f32[131072,5]{1,0:T(8,128)}) %all-gather.3.cloned.1.call-update) | async-done | bytes 2621456 | tf_op jit(solution)/shard_map/all_gather | solution.py:159
  571.1 321.9 %scatter_custom_fusion.1 = f32[16384,5]{1,0:T(8,128)} fusion(s32[131072]{0:T(1024)S(1)} %compare_select_fusion, f32[131072,5]{1,0:T(8,128)} %all-gather.3.cloned.1.call-done, f32[]{:T(128)} %constant.124.clone.1), kind=kCustom, calls=%fused_computation.6 | custom fusion | bytes 328192 | tf_op jit(solution)/shard_map/scatter | solution.py:171
  893.0 6.0 copy.31
  (52 shorter events, 0.4 us)
Async XLA Ops:
  7.2 27.7 %copy-start.14 = (f32[16,6,64,1]{2,0,3,1:T(8,128)S(1)}, f32[16,6,64,1]{2,0,3,1:T(8,128)}, u32[]{:S(2)}) copy-start(f32[16,6,64,1]{2,0,3,1:T(8,128)} %constant.160) | copy-start | bytes 73732
  7.2 563.9 %all-gather.3.cloned.1.call-start = ((), (), s32[]{:S(2)}) async-start(), calls=%async_computation | async-start | bytes 71303168 | tf_op jit(solution)/shard_map/all_gather | solution.py:159
  34.9 11.1 %copy-start = (f32[6,1024,16]{2,1,0:T(8,128)}, f32[6,1024,16]{2,1,0:T(8,128)S(1)}, u32[]{:S(2)}) copy-start(f32[6,1024,16]{2,1,0:T(8,128)S(1)} %copy.19) | copy-start | bytes 1179652
  38.9 3.7 copy-start.2
  46.0 10.0 %copy-start.10 = (s32[6,1024]{1,0:T(8,128)S(1)}, s32[6,1024]{1,0:T(8,128)}, u32[]{:S(2)}) copy-start(s32[6,1024]{1,0:T(8,128)} %param.15) | copy-start | bytes 73732
  46.0 10.0 %copy-start.11 = (s32[8192]{0:T(1024)S(1)}, s32[8192]{0:T(1024)}, u32[]{:S(2)}) copy-start(s32[8192]{0:T(1024)} %param.16) | copy-start | bytes 98308
  46.0 10.7 %copy-start.13 = (f32[3,8192]{1,0:T(4,128)S(1)}, f32[3,8192]{1,0:T(4,128)}, u32[]{:S(2)}) copy-start(f32[3,8192]{1,0:T(4,128)} %param.17) | copy-start | bytes 294916
  46.0 11.9 %copy-start.12 = (f32[3,64,64,1]{2,1,3,0:T(8,128)S(1)}, f32[3,64,64,1]{2,1,3,0:T(8,128)}, u32[]{:S(2)}) copy-start(f32[3,64,64,1]{2,1,3,0:T(8,128)} %constant.159) | copy-start | bytes 147460
  46.0 11.9 %copy-start.17 = (f32[3,1024]{1,0:T(4,128)S(1)}, f32[3,1024]{1,0:T(4,128)}, u32[]{:S(2)}) copy-start(f32[3,1024]{1,0:T(4,128)} %param.12) | copy-start | bytes 36868
  50.6 7.3 copy-start.4
  53.3 34.6 %collective-permute-start = (f32[64,96]{1,0:T(8,128)S(1)}, f32[64,96]{1,0:T(8,128)S(1)}, u32[]{:S(2)}, u32[]{:S(2)}) collective-permute-start(f32[64,96]{1,0:T(8,128)S(1)} %get-tuple-element.18), channel_id=1, source_target_pairs={{0,16},{16,32},{32,48},{48,64},{64,80},{80,96},{96,112},{112,0},{1... | collective-permute-start | bytes 73736 | tf_op jit(solution)/shard_map/ppermute | solution.py:19
  56.0 32.5 %collective-permute-start.1 = (f32[64,96]{1,0:T(8,128)S(1)}, f32[64,96]{1,0:T(8,128)}, u32[]{:S(2)}, u32[]{:S(2)}) collective-permute-start(f32[64,96]{1,0:T(8,128)S(1)} %get-tuple-element.19), channel_id=1, source_target_pairs={{16,0},{32,16},{48,32},{64,48},{80,64},{96,80},{112,96},{0,112},{1... | collective-permute-start | bytes 73736 | tf_op jit(solution)/shard_map/ppermute | solution.py:20
  57.8 5.2 copy-start.16
  57.9 27.1 %copy-start.7 = (f32[16,6,1024]{2,1,0:T(8,128)S(1)}, f32[16,6,1024]{2,1,0:T(8,128)}, u32[]{:S(2)}) copy-start(f32[16,6,1024]{2,1,0:T(8,128)} %reshape.165) | copy-start | bytes 1179652
  57.9 28.0 %copy-start.9 = (f32[64,1024]{1,0:T(8,128)S(1)}, f32[64,1024]{1,0:T(8,128)}, u32[]{:S(2)}) copy-start(f32[64,1024]{1,0:T(8,128)} %param.13) | copy-start | bytes 786436
  88.0 0.6 copy-start.15
  113.4 4.8 copy-start.1
  127.2 6.2 copy-start.3
  127.2 6.2 copy-start.5
  177.5 12.1 %copy-start.6 = (f32[64,8192]{1,0:T(8,128)S(1)}, f32[64,8192]{1,0:T(8,128)}, u32[]{:S(2)}) copy-start(f32[64,8192]{1,0:T(8,128)} %mul.255) | copy-start | bytes 6291460
  197.9 1.0 copy-start.8
Sparse Core Ops, SparseCore 0:
  198.1 372.9 all-gather.2
where the time goes:
time: 907 us; the launch traced here: 906 us
  local copies, waits for them, and re-layouts  455 us (50%)
  waiting for transfers between devices  365 us (40%)
  other arithmetic  30.8 us (3%)
  blocking collectives  22 us (2%)
  matrix products  15.8 us (2%)
  between operations  14.4 us (2%)
    all_gather x1, waiting for transfers between devices, on_device(): lax.all_gather(receptor_vals, 'bulk', axis=0, tiled=True)  365 us
    scatter x1, local copies, waits for them, and re-layouts, on_device(): fringe_rows = fringe_rows.at[places].set(gathered_vals, mode='drop')  322 us
    gather x2, local copies, waits for them, and re-layouts, receptor_rows(): jnp.take(element_rows, donors, axis=0).reshape(donors.shape[0], nvars, 64)  46.9 us
    scatter x1, local copies, waits for them, and re-layouts, rim_rows(): senders = jnp.zeros((2 * rim_count,), jnp.int32).at[slots].set(jnp.arange...  23 us
    all_gather x1, blocking collectives, on_device(): lax.all_gather(owners, 'bulk', axis=0, tiled=True)  22 us
    gather x1, local copies, waits for them, and re-layouts, surface_term(): outer = jnp.take(full_table, links, axis=0)  21.1 us
  transfers between devices with their start and end apart: 3, of which 1 were waited for; matrix products, arithmetic and copies ran while one was open for 2% of the time, Pallas kernels for 0%

commit v1 on v0

--- a/solution.py
+++ b/solution.py
@@ -7,6 +7,15 @@
 gauss_nodes = (-0.8611363115940526, -0.3399810435848563, 0.3399810435848563, 0.8611363115940526)
 quad_weights = (0.3478548451374538, 0.6521451548625461, 0.6521451548625461, 0.3478548451374538)
 section_step = 0.2
+write_body_by_axis = lambda a0, axis_k: jnp.concatenate(
+    lax.all_to_all(
+        jnp.stack([a0 for _ in range(lax.axis_size("bulk"))]),
+        axis_name="bulk",
+        split_axis=0,
+        concat_axis=0,
+    ),
+    axis=axis_k,
+)
 
 
 def padded(shard, sides, width):
@@ -156,7 +165,7 @@
     capacity = 2 * receptors // buckets
     owners = owner_list[:, 0]
     gathered_vals, gathered_owners = (
-        lax.all_gather(receptor_vals, "bulk", axis=0, tiled=True),
+        write_body_by_axis(receptor_vals, 0),
         lax.all_gather(owners, "bulk", axis=0, tiled=True),
     )
     by_source = gathered_owners.reshape(buckets, receptors)

time: 907 us -> 620 us (0.68); the launches traced: 906 us -> 610 us
  waiting for transfers between devices: 365 us -> 46.1 us
  local copies, waits for them, and re-layouts: 455 us -> 486 us
  between operations: 14.4 us -> 1.01 us
    all_gather x1 -> x0, waiting for transfers between devices: 365 us -> none  [on_device(): lax.all_gather(receptor_vals, 'bulk', axis=0, tiled=True)]
    all_to_all x0 -> x1, waiting for transfers between devices: none -> 46.1 us  [lax.all_to_all(jnp.stack([a0 for _ in range(lax.axis_size('bulk'))]), axi...]
    reshape x0 -> x1, local copies, waits for them, and re-layouts: none -> 30.4 us  [jnp.concatenate(lax.all_to_all(jnp.stack([a0 for _ in range(lax.axis_size...]
  transfers between devices with their start and end apart: 3 -> 3, of which waited for: 1 -> 1; matrix products, arithmetic and copies ran while one was open for 2% -> 3% of each run, Pallas kernels for 0% -> 0%
where the time goes in v1:
time: 620 us; the launch traced here: 610 us
  local copies, waits for them, and re-layouts  486 us (78%)
  waiting for transfers between devices  46.1 us (7%)
  other arithmetic  32.1 us (5%)
  blocking collectives  20.4 us (3%)
  matrix products  16.6 us (3%)
  starting transfers between devices  7.6 us (1%)
    scatter x1, local copies, waits for them, and re-layouts, on_device(): fringe_rows = fringe_rows.at[places].set(gathered_vals, mode='drop')  322 us
    gather x2, local copies, waits for them, and re-layouts, receptor_rows(): jnp.take(element_rows, donors, axis=0).reshape(donors.shape[0], nvars, 64)  46.9 us
    all_to_all x1, waiting for transfers between devices, lax.all_to_all(jnp.stack([a0 for _ in range(lax.axis_size('bulk'))]), axi...  46.1 us
    reshape x1, local copies, waits for them, and re-layouts, jnp.concatenate(lax.all_to_all(jnp.stack([a0 for _ in range(lax.axis_size...  30.4 us
    scatter x1, local copies, waits for them, and re-layouts, rim_rows(): senders = jnp.zeros((2 * rim_count,), jnp.int32).at[slots].set(jnp.arange...  23 us
    gather x1, local copies, waits for them, and re-layouts, surface_term(): outer = jnp.take(full_table, links, axis=0)  21.1 us
    all_gather x1, blocking collectives, on_device(): lax.all_gather(owners, 'bulk', axis=0, tiled=True)  20.4 us
  transfers between devices with their start and end apart: 3, of which 1 were waited for; matrix products, arithmetic and copies ran while one was open for 3% of the time, Pallas kernels for 0%

profile of v1, /device:TPU:1, one launch (start us, length us, event | category | flops | bytes accessed | tf_op | source)
XLA Modules:
  0.0 609.7 jit_solution(16229186019303480778)
XLA Ops:
  0.6 0.8 copy.68
  1.5 23.0 %scatter_custom_fusion = s32[128]{0:T(128)S(1)} fusion(s32[6144]{0:T(1024)S(1)} %bitcast.88, s32[6144]{0:T(1024)S(1)} %iota.8, s32[]{:T(128)} %constant.125.clone.1), kind=kCustom, calls=%fused_computation.82 | custom fusion | bytes 516 | tf_op jit(solution)/shard_map/scatter | solution.py:106
  24.5 1.8 reshape.170
  26.4 1.9 copy.44
  28.3 4.0 convolution_bitcast_fusion
  32.3 1.2 copy.45
  33.5 2.5 copy.67
  36.1 3.4 copy.46
  39.4 4.5 pad_maximum_fusion.1
  44.0 2.5 gather_fusion
  46.6 0.6 fusion.28
  47.2 2.7 collective-permute-start
  50.0 0.6 fusion.25
  50.6 0.8 multiply_multiply_fusion.11
  51.4 0.9 broadcast_bitcast_fusion
  52.3 20.4 %all-gather = s32[131072,1]{0,1:T(1,128)S(1)} all-gather(s32[8192,1]{0,1:T(1,128)S(1)} %copy-done.20), channel_id=2, replica_groups=mesh['valve'=8,'bulk'=16] {'bulk'}, dimensions={0}, use_global_device_ids=true | all-gather | bytes 557056 | tf_op jit(solution)/shard_map/all_gather | solution.py:169
  72.7 0.5 compare_convert_fusion
  73.2 0.8 copy-done.8
  74.0 4.8 reduce-window.6
  78.8 0.5 slice_reduce_fusion
  79.3 0.2 reduce-window.9
  79.5 1.0 broadcast_add_fusion
  80.6 0.2 pad_maximum_fusion.2
  81.1 0.5 broadcast_multiply_fusion.1
  81.7 5.2 multiply_reduce_fusion.1
  86.9 1.0 copy.52
  87.8 0.7 neg.4
  88.6 0.9 copy.69
  89.5 1.7 mul.255
  91.2 3.8 pad_maximum_fusion
  95.0 21.1 %gather_fusion.1 = f32[6144,96]{1,0:T(8,128)} fusion(f32[6272,96]{1,0:T(8,128)S(1)} %pad_maximum_fusion, s32[6144]{0:T(1024)S(1)} %broadcast_clamp_fusion), kind=kCustom, calls=%fused_computation.1 | custom fusion | bytes 4743168 | tf_op jit(solution)/shard_map/jit(_take)/gather | solution.py:114
  116.0 4.8 broadcast_select_fusion
  120.9 3.5 broadcast_multiply_fusion
  124.3 2.2 copy.48
  126.5 3.4 reshape.174
  129.9 3.1 copy.47
  133.0 3.0 copy.50
  136.1 7.4 %multiply_add_fusion = (f32[5,64,1024]{2,1,0:T(8,128)}, f32[5,64,1024]{2,1,0:T(8,128)}) fusion(f32[5,64,1024]{2,1,0:T(8,128)S(1)} %copy-done.5, f32[64,16,6,1]{0,1,3,2:T(8,128)} %constant.161, f32[6,1024,16,5]{1,2,3,0:T(8,128)S(1)} %copy-done.3, f32[6,1024,16,5]{1,0,3,2:T(8,128)} %reshape.174, f32[6,1024,16]{1,2,0:T(8,128)} %copy.52, ...), kind=kOutput, calls=%fused_computation.32 | convolution fusion | flops 382238720 | bytes 10641408 | tf_op jit(solution)/shard_map/pqf,feqv->vpe/dot_general | solution.py:122
  143.5 1.8 copy.53
  145.3 34.9 %gather_fusion.2 = f32[8192,320]{1,0:T(8,128)} fusion(f32[1024,320]{1,0:T(8,128)S(1)} %copy.53, s32[8192]{0:T(1024)} %fusion.25), kind=kCustom, calls=%fused_computation.2 | custom fusion | bytes 21004288 | tf_op jit(solution)/shard_map/jit(_take)/gather | solution.py:140
  180.1 12.1 %copy.54 = f32[8192,320]{0,1:T(8,128)} copy(f32[8192,320]{1,0:T(8,128)} %gather_fusion.2) | data formatting | bytes 20971520 | tf_op jit(solution)/shard_map/jit(_take)/gather | solution.py:140
  192.2 5.7 multiply_reduce_fusion
  197.9 2.4 stack.11
  200.3 4.9 all-to-all-start
  205.3 46.1 %all-to-all-done = f32[16,8192,5]{1,2,0:T(8,128)} async-done(((f32[16,8192,5]{1,2,0:T(8,128)}), f32[16,8192,5]{1,2,0:T(8,128)}, u32[]{:S(2)}, u32[]{:S(2)}) %all-to-all-start) | async-done | bytes 2621472 | tf_op jit(solution)/shard_map/all_to_all | solution.py:11
  251.5 30.4 %copy.55 = f32[131072,5]{1,0:T(8,128)} copy(f32[131072,5]{0,1:T(8,128)} %bitcast.25) | data formatting | bytes 5242880 | tf_op jit(solution)/shard_map/reshape | solution.py:10
  281.9 321.9 %scatter_custom_fusion.1 = f32[16384,5]{1,0:T(8,128)} fusion(s32[131072]{0:T(1024)S(1)} %compare_select_fusion, f32[131072,5]{1,0:T(8,128)} %copy.55, f32[]{:T(128)} %constant.124.clone.1), kind=kCustom, calls=%fused_computation.6 | custom fusion | bytes 328192 | tf_op jit(solution)/shard_map/scatter | solution.py:180
  603.7 6.0 copy.56
  (58 shorter events, 0.7 us)
Async XLA Ops:
  0.6 27.7 %copy-start.19 = (f32[16,6,64,1]{2,0,3,1:T(8,128)S(1)}, f32[16,6,64,1]{2,0,3,1:T(8,128)}, u32[]{:S(2)}) copy-start(f32[16,6,64,1]{2,0,3,1:T(8,128)} %constant.160) | copy-start | bytes 73732
  28.3 11.1 %copy-start = (f32[6,1024,16]{2,1,0:T(8,128)}, f32[6,1024,16]{2,1,0:T(8,128)S(1)}, u32[]{:S(2)}) copy-start(f32[6,1024,16]{2,1,0:T(8,128)S(1)} %copy.44) | copy-start | bytes 1179652
  32.3 3.7 copy-start.2
  39.4 10.5 %copy-start.15 = (s32[6,1024]{1,0:T(8,128)S(1)}, s32[6,1024]{1,0:T(8,128)}, u32[]{:S(2)}) copy-start(s32[6,1024]{1,0:T(8,128)} %param.15) | copy-start | bytes 73732
  39.4 10.5 %copy-start.16 = (s32[8192]{0:T(1024)S(1)}, s32[8192]{0:T(1024)}, u32[]{:S(2)}) copy-start(s32[8192]{0:T(1024)} %param.16) | copy-start | bytes 98308
  39.4 11.2 %copy-start.18 = (f32[3,8192]{1,0:T(4,128)S(1)}, f32[3,8192]{1,0:T(4,128)}, u32[]{:S(2)}) copy-start(f32[3,8192]{1,0:T(4,128)} %param.17) | copy-start | bytes 294916
  39.4 12.9 %copy-start.20 = (s32[8192,1]{0,1:T(1,128)S(1)}, s32[8192,1]{0,1:T(1,128)}, u32[]{:S(2)}) copy-start(s32[8192,1]{0,1:T(1,128)} %param.18) | copy-start | bytes 98308
  47.2 44.0 %collective-permute-start = (f32[64,96]{1,0:T(8,128)}, f32[64,96]{1,0:T(8,128)}, u32[]{:S(2)}, u32[]{:S(2)}) collective-permute-start(f32[64,96]{1,0:T(8,128)} %get-tuple-element.22), channel_id=1, source_target_pairs={{0,16},{16,32},{32,48},{48,64},{64,80},{80,96},{96,112},{112,0},{1... | collective-permute-start | bytes 73736 | tf_op jit(solution)/shard_map/ppermute | solution.py:28
  49.9 41.3 %collective-permute-start.1 = (f32[64,96]{1,0:T(8,128)}, f32[64,96]{1,0:T(8,128)}, u32[]{:S(2)}, u32[]{:S(2)}) collective-permute-start(f32[64,96]{1,0:T(8,128)} %get-tuple-element.23), channel_id=1, source_target_pairs={{16,0},{32,16},{48,32},{64,48},{80,64},{96,80},{112,96},{0,112},{1... | collective-permute-start | bytes 73736 | tf_op jit(solution)/shard_map/ppermute | solution.py:29
  73.2 0.8 copy-start.8
  78.8 2.9 copy-start.4
  78.8 2.9 copy-start.17
  80.8 6.0 copy-start.7
  81.1 6.8 %copy-start.14 = (f32[64,1024]{1,0:T(8,128)S(1)}, f32[64,1024]{1,0:T(8,128)}, u32[]{:S(2)}) copy-start(f32[64,1024]{1,0:T(8,128)} %param.13) | copy-start | bytes 786436
  81.1 7.5 %copy-start.10 = (s32[2,64,8,128]{3,2,1,0:T(8,128)S(1)}, s32[2,64,8,128]{3,2,1,0:T(8,128)}, u32[]{:S(2)}) copy-start(s32[2,64,8,128]{3,2,1,0:T(8,128)} %broadcast_bitcast_fusion) | copy-start | bytes 1572868
  116.0 4.8 copy-start.1
  129.9 6.2 %copy-start.3 = (f32[6,1024,16,5]{1,2,3,0:T(8,128)S(1)}, f32[6,1024,16,5]{1,2,3,0:T(8,128)}, u32[]{:S(2)}) copy-start(f32[6,1024,16,5]{1,2,3,0:T(8,128)} %copy-done.2) | copy-start | bytes 5898244
  129.9 6.2 %copy-start.5 = (f32[5,64,1024]{2,1,0:T(8,128)S(1)}, f32[5,64,1024]{2,1,0:T(8,128)}, u32[]{:S(2)}) copy-start(f32[5,64,1024]{2,1,0:T(8,128)} %param.11) | copy-start | bytes 3932164
  129.9 6.2 %copy-start.13 = (f32[64,1024]{1,0:T(8,128)S(1)}, f32[64,1024]{1,0:T(8,128)}, u32[]{:S(2)}) copy-start(f32[64,1024]{1,0:T(8,128)} %neg.4) | copy-start | bytes 786436
  180.1 12.1 %copy-start.6 = (f32[64,8192]{1,0:T(8,128)S(1)}, f32[64,8192]{1,0:T(8,128)}, u32[]{:S(2)}) copy-start(f32[64,8192]{1,0:T(8,128)} %mul.255) | copy-start | bytes 6291460
  200.2 4.9 copy-start.9
  200.2 4.9 copy-start.11
  200.3 5.0 copy-start.12
  200.3 51.2 %all-to-all-start = ((f32[16,8192,5]{1,2,0:T(8,128)}), f32[16,8192,5]{1,2,0:T(8,128)}, u32[]{:S(2)}, u32[]{:S(2)}) async-start(f32[16,8192,5]{1,2,0:T(8,128)} %stack.11), calls=%async_computation | async-start | bytes 8388608 | tf_op jit(solution)/shard_map/all_to_all | solution.py:11
